TPU v7x, 32 devices: a whole 2x2x4 slice. The times are simulated.
32 devices in a mesh: req: 8 (over y, x, core), kv: 4 (over z).
Axes of the slice: x: 2, y: 2, z: 4, core: 2. Of those that a mesh axis runs over, the one named last changes fastest.
Arguments:
- hidden: bfloat16 [128, 8192], P('req', 'kv')
- cache_len: int32 [2, 128], replicated, may hold values from 1 to 4096, as said below
- request_serving_order: int32 [128], replicated, may hold values from 0 to 127, as said below
- rotated_key_cache: bfloat16 [2, 65536, 1024], P(None, 'req', 'kv'), as said below
- stored_value_cache: bfloat16 [2, 65536, 1024], P(None, 'req', 'kv'), may hold values from -6 to 6
- attn_gain: bfloat16 [8192], P('kv'), may hold values from 0.099609375 to 1.8984375
- w_query: bfloat16 [8192, 8192], P('req', 'kv'), may hold values from -0.0625 to 0.0625
- key_projection_weight: bfloat16 [8192, 1024], P('req', 'kv'), may hold values from -0.0625 to 0.0625
- value_projection_weight: bfloat16 [8192, 1024], P('req', 'kv'), may hold values from -0.0625 to 0.0625
- b_query: bfloat16 [8192], P('kv'), may hold values from -3 to 3
- key_bias: bfloat16 [1024], P('kv'), may hold values from -4.5 to 4.5
- value_bias: bfloat16 [1024], P('kv'), may hold values from -4.5 to 4.5
- w_out: bfloat16 [8192, 8192], P('req', 'kv'), may hold values from -0.0625 to 0.0625
- mlp_gain: bfloat16 [8192], P('kv'), may hold values from 0.099609375 to 1.8984375
- w_gate: bfloat16 [8192, 29568], P('kv', 'req'), may hold values from -0.0625 to 0.0625
- w_up: bfloat16 [8192, 29568], P('kv', 'req'), may hold values from -0.0625 to 0.0625
- w_down: bfloat16 [29568, 8192], P('req', 'kv'), may hold values from -0.03125 to 0.03125
Outputs:
- residual: float32 [128, 8192], P('req', 'kv')
Inputs may be any that keep to these rules, and one draw needn't show every extreme that they name: `request_serving_order`: A permutation of the requests. `cache_len`: in each layer the caches of the requests of one serving index of req sum to at most 8192 rows, and to exactly 8192 for one index; some request of that index has exactly 4096. `rotated_key_cache`: rows of an index beyond its requests' caches hold no cached tokens.
All inputs are finite; a program needn't handle non-finite values.
Results may differ from a plain program's by a relative error of at most 0.015.
Values may be sent and summed in bfloat16 or wider, within the bound.
No kernel may reach another device: no remote copies, remote signals or barrier semaphores. Data moves between devices by JAX's collectives and lax.ppermute only.
A program may use at most 256 MiB of HBM per device.

v0:
```python
import math
import jax
import jax.numpy as jnp
from jax import lax
from jax.sharding import PartitionSpec as P

MODEL_WIDTH = 8192
HEAD_SIZE = 128
LAYER_COUNT = 2
EPS = 1e-06
LOG_BASE = math.log(1000000.0)


def scatter_sum(block, axis):
    count = lax.axis_size(axis)
    index = lax.axis_index(axis)
    chunks = block.reshape(count, block.shape[0] // count, *block.shape[1:])
    total = jnp.take(chunks, index, axis=0)
    for shift in range(1, count):
        piece = jnp.take(chunks, (index + shift) % count, axis=0)
        total = total + lax.ppermute(piece, axis, [(j, (j + shift) % count) for j in range(count)])
    return total


def rows_for_weights(block):
    wide = lax.all_gather(block, "kv", axis=1, tiled=True)
    return lax.all_to_all(wide, "req", 1, 0, tiled=True)


def apply_rotation(values, token_positions):
    half_width = values.shape[-1] // 2
    frequency = jnp.exp(
        -LOG_BASE * jnp.arange(half_width, dtype=jnp.float32) * 2.0 / values.shape[-1]
    )
    angles = token_positions[:, None] * frequency[None, :]
    reshape_to = (angles.shape[0],) + (1,) * (values.ndim - 2) + (half_width,)
    cosine = jnp.cos(angles).reshape(reshape_to)
    sine_part = jnp.sin(angles).reshape(reshape_to)
    front_half = values[..., :half_width]
    back_half = values[..., half_width:]
    return jnp.concatenate(
        [front_half * cosine - back_half * sine_part, back_half * cosine + front_half * sine_part],
        axis=-1,
    )


def normalize(residual, gains):
    square_sum = jnp.sum(residual * residual, axis=1)
    all_squares = lax.psum(square_sum, "kv")
    inv_norm = lax.rsqrt(all_squares / MODEL_WIDTH + EPS)
    return (residual * inv_norm[:, None] * gains.astype(jnp.float32)[None, :]).astype(jnp.bfloat16)


def attend(query_rows, fresh_key, fresh_value, cached_keys, cached_values, lengths):
    score_scale = 1.0 / math.sqrt(query_rows.shape[-1])
    finish = jnp.cumsum(lengths)
    starts = finish - lengths
    capacity = cached_keys.shape[0]
    block_size = min(512, capacity)
    block_count = capacity // block_size
    self_score = (
        jnp.einsum("igrd,igd->igr", query_rows, fresh_key, preferred_element_type=jnp.float32)
        * score_scale
    )
    start_out = fresh_value.astype(jnp.float32)[:, :, None, :] * jnp.ones(
        query_rows.shape, jnp.float32
    )

    def one_block(block_index, carried):
        running_max, running_sum, accumulated = carried
        first_row = block_index * block_size
        key_block = lax.dynamic_slice_in_dim(cached_keys, first_row, block_size, 0)
        value_block = lax.dynamic_slice_in_dim(cached_values, first_row, block_size, 0)
        scores = (
            jnp.einsum("igrd,tgd->igrt", query_rows, key_block, preferred_element_type=jnp.float32)
            * score_scale
        )
        key_rows = first_row + jnp.arange(block_size, dtype=jnp.int32)
        inside = (key_rows[None, :] >= starts[:, None]) & (key_rows[None, :] < finish[:, None])
        inside = inside[:, None, None, :]
        block_max = jnp.max(jnp.where(inside, scores, -jnp.inf), axis=-1)
        new_max = jnp.maximum(running_max, block_max)
        exps = jnp.where(inside, jnp.exp(scores - new_max[..., None]), 0.0)
        rescale = jnp.exp(running_max - new_max)
        new_sum = running_sum * rescale + jnp.sum(exps, axis=-1)
        contribution = jnp.einsum(
            "igrt,tgd->igrd",
            exps.astype(jnp.bfloat16),
            value_block,
            preferred_element_type=jnp.float32,
        )
        return (new_max, new_sum, accumulated * rescale[..., None] + contribution)

    running_max, running_sum, accumulated = lax.fori_loop(
        0, block_count, one_block, (self_score, jnp.ones_like(self_score), start_out)
    )
    return (accumulated / running_sum[..., None]).astype(jnp.bfloat16)


def body(
    hidden,
    cache_len,
    request_serving_order,
    rotated_key_cache,
    stored_value_cache,
    attn_gain,
    w_query,
    key_projection_weight,
    value_projection_weight,
    b_query,
    key_bias,
    value_bias,
    w_out,
    mlp_gain,
    w_gate,
    w_up,
    w_down,
):
    req_size = lax.axis_size("req")
    kv_size = lax.axis_size("kv")
    group_ratio = req_size // kv_size
    req_index = lax.axis_index("req")
    own_rows = hidden.shape[0]
    head_dim = HEAD_SIZE
    query_width = w_query.shape[1]
    key_width = key_projection_weight.shape[1]
    kv_heads = key_width // head_dim
    capacity = rotated_key_cache.shape[1]
    w_joint = jnp.concatenate([w_query, key_projection_weight, value_projection_weight], axis=1)
    b_joint = jnp.concatenate([b_query, key_bias, value_bias]).astype(jnp.float32)
    inverse = jnp.argsort(request_serving_order)
    my_slots = lax.dynamic_slice_in_dim(request_serving_order, req_index * own_rows, own_rows)
    residual = hidden.astype(jnp.float32)
    for current_layer_index in range(LAYER_COUNT):
        normed = normalize(residual, attn_gain)
        columns = rows_for_weights(normed)
        picked = jnp.take(columns, request_serving_order, axis=0)
        combined = (
            scatter_sum(jnp.dot(picked, w_joint, preferred_element_type=jnp.float32), "req")
            + b_joint[None, :]
        )
        lengths = jnp.take(cache_len[current_layer_index], my_slots)
        token_positions = lengths.astype(jnp.float32)
        query_rows = apply_rotation(
            combined[:, :query_width].reshape(own_rows, kv_heads, -1, head_dim), token_positions
        ).astype(jnp.bfloat16)
        fresh_key = apply_rotation(
            combined[:, query_width : query_width + key_width].reshape(
                own_rows, kv_heads, head_dim
            ),
            token_positions,
        ).astype(jnp.bfloat16)
        fresh_value = (
            combined[:, query_width + key_width :]
            .reshape(own_rows, kv_heads, head_dim)
            .astype(jnp.bfloat16)
        )
        cached_keys = rotated_key_cache[current_layer_index].reshape(capacity, kv_heads, head_dim)
        cached_values = stored_value_cache[current_layer_index].reshape(
            capacity, kv_heads, head_dim
        )
        attention_output = attend(
            query_rows, fresh_key, fresh_value, cached_keys, cached_values, lengths
        ).reshape(own_rows, query_width)
        head_rows = rows_for_weights(attention_output)
        project_picked = jnp.take(head_rows, inverse, axis=0)
        residual = residual + scatter_sum(
            jnp.dot(project_picked, w_out, preferred_element_type=jnp.float32), "req"
        )
        normed_mlp = normalize(residual, mlp_gain)
        tokens = lax.all_gather(normed_mlp, "req", axis=0, tiled=True)
        hidden_cols = w_gate.shape[1]
        gate_up = lax.psum_scatter(
            jnp.concatenate(
                [
                    jnp.dot(tokens, w_gate, preferred_element_type=jnp.float32),
                    jnp.dot(tokens, w_up, preferred_element_type=jnp.float32),
                ],
                axis=1,
            ),
            "kv",
            scatter_dimension=0,
            tiled=True,
        )
        local_hidden = (jax.nn.silu(gate_up[:, :hidden_cols]) * gate_up[:, hidden_cols:]).astype(
            jnp.bfloat16
        )
        hidden_all = lax.all_gather(local_hidden, "kv", axis=0, tiled=True)
        residual = residual + scatter_sum(
            jnp.dot(hidden_all, w_down, preferred_element_type=jnp.float32), "req"
        )
    return residual


def solution(mesh):
    return jax.shard_map(
        body,
        mesh=mesh,
        in_specs=(
            P("req", "kv"),
            P(),
            P(),
            P(None, "req", "kv"),
            P(None, "req", "kv"),
            P("kv"),
            P("req", "kv"),
            P("req", "kv"),
            P("req", "kv"),
            P("kv"),
            P("kv"),
            P("kv"),
            P("req", "kv"),
            P("kv"),
            P("kv", "req"),
            P("kv", "req"),
            P("req", "kv"),
        ),
        out_specs=P("req", "kv"),
        check_vma=False,
    )
```

profile of v0, /device:TPU:1, one launch (start us, length us, event | category | flops | bytes accessed | tf_op | source)
XLA Modules:
  0.0 656.0 jit_solution(5651597795348831521)
XLA Ops:
  8.2 10.8 %psum.28 = f32[16]{0:T(128)S(1)} all-reduce(f32[16]{0:T(128)S(1)} %fusion.60), channel_id=1, replica_groups=mesh['req'=8,'kv'=4] {'kv'}, use_global_device_ids=true, to_apply=%region_1.2 | all-reduce | flops 16 | bytes 128 | tf_op jit(solution)/shard_map/psum | solution.py:49
  19.9 11.1 %all_gather.24 = bf16[16,8192]{1,0:T(8,128)(2,1)S(1)} all-gather(bf16[16,2048]{1,0:T(8,128)(2,1)S(1)} %fusion.62), channel_id=1, replica_groups=mesh['req'=8,'kv'=4] {'kv'}, dimensions={1}, use_global_device_ids=true | all-gather | bytes 327680 | tf_op jit(solution)/shard_map/all_gather | solution.py:26
  31.7 9.2 %all-to-all-start = ((bf16[16,8,1024]{2,0,1:T(8,128)(2,1)}), bf16[16,8,1024]{2,0,1:T(8,128)(2,1)S(1)}, u32[]{:S(2)}, u32[]{:S(2)}) async-start(bf16[16,8,1024]{2,0,1:T(8,128)(2,1)} %bitcast.324), calls=%async_computation | async-start | bytes 524288 | tf_op jit(solution)/shard_map/all_to_all | solution.py:27
  48.5 5.7 fusion.111
  54.2 5.9 fusion.110
  78.8 6.4 copy.106
  85.2 6.5 copy.107
  92.6 46.3 %while.38 = (s32[]{:T(128)}, f32[16,2,8]{0,2,1:T(8,128)S(1)}, f32[16,2,8]{0,2,1:T(8,128)S(1)}, f32[16,2,8,128]{3,0,2,1:T(8,128)S(1)}, s32[16]{0:T(128)S(1)}, /*i...) while((s32[]{:T(128)}, f32[16,2,8]{0,2,1:T(8,128)S(1)}, ...), condition=%wide.region_6.10_spmd.clone, body=%wide.region_3.9_spmd.clone.sunk | while | flops 68379904 | bytes 2478401 | solution.py:94
  139.1 11.4 %all_gather.25 = bf16[16,8192]{1,0:T(8,128)(2,1)S(1)} all-gather(bf16[16,2048]{1,0:T(8,128)(2,1)S(1)} %bitcast.371), channel_id=1, replica_groups=mesh['req'=8,'kv'=4] {'kv'}, dimensions={1}, use_global_device_ids=true | all-gather | bytes 327680 | tf_op jit(solution)/shard_map/all_gather | solution.py:26
  151.2 8.5 %all-to-all-start.1 = ((bf16[16,8,1024]{2,0,1:T(8,128)(2,1)}), bf16[16,8,1024]{2,0,1:T(8,128)(2,1)S(1)}, u32[]{:S(2)}, u32[]{:S(2)}) async-start(bf16[16,8,1024]{2,0,1:T(8,128)(2,1)} %bitcast.323), calls=%async_computation.1 | async-start | bytes 524288 | tf_op jit(solution)/shard_map/all_to_all | solution.py:27
  186.0 7.1 %psum.29 = f32[16]{0:T(128)S(1)} all-reduce(f32[16]{0:T(128)S(1)} %get-tuple-element.505), channel_id=1, replica_groups=mesh['req'=8,'kv'=4] {'kv'}, use_global_device_ids=true, to_apply=%region_9.14 | all-reduce | flops 16 | bytes 128 | tf_op jit(solution)/shard_map/psum | solution.py:49
  193.2 13.0 %all_gather.26 = bf16[128,2048]{1,0:T(8,128)(2,1)S(1)} all-gather(bf16[16,2048]{1,0:T(8,128)(2,1)S(1)} %multiply_convert_fusion.2), channel_id=1, replica_groups=mesh['req'=8,'kv'=4] {'req'}, dimensions={0}, use_global_device_ids=true | all-gather | bytes 589824 | tf_op jit(solution)/shard_map/all_gather | solution.py:171
  206.2 7.6 %fusion.112 = f32[128,3696]{0,1:T(8,128)S(1)} fusion(bf16[128,2048]{1,0:T(8,128)(2,1)S(1)} %all_gather.26, bf16[2048,3696]{0,1:T(8,128)(2,1)} %param.43), kind=kOutput, calls=%fused_computation.247 | convolution fusion | flops 1937768448 | bytes 17555456 | tf_op jit(solution)/shard_map/dot_general | solution.py:176
  213.8 7.6 %fusion.113 = f32[128,3696]{0,1:T(8,128)S(1)} fusion(bf16[128,2048]{1,0:T(8,128)(2,1)S(1)} %all_gather.26, bf16[2048,3696]{0,1:T(8,128)(2,1)} %param.44), kind=kOutput, calls=%fused_computation.248 | convolution fusion | flops 1937768448 | bytes 17555456 | tf_op jit(solution)/shard_map/dot_general | solution.py:177
  228.9 67.8 %reduce-scatter.7.cloned.1.call-done = f32[32,7392]{1,0:T(8,128)} async-done(((f32[128,7392]{1,0:T(8,128)}), f32[32,7392]{1,0:T(8,128)}) %reduce-scatter.7.cloned.1.call-update) | async-done | bytes 946192 | tf_op jit(solution)/shard_map/reduce_scatter | solution.py:173
  298.1 19.2 %all_gather.27 = bf16[128,3696]{1,0:T(8,128)(2,1)S(1)} all-gather(bf16[32,3696]{1,0:T(8,128)(2,1)S(1)} %fusion.33), channel_id=1, replica_groups=mesh['req'=8,'kv'=4] {'kv'}, dimensions={0}, use_global_device_ids=true | all-gather | bytes 1182720 | tf_op jit(solution)/shard_map/all_gather | solution.py:188
  317.3 7.7 %fusion.114 = f32[128,2048]{1,0:T(8,128)S(1)} fusion(bf16[128,3696]{1,0:T(8,128)(2,1)S(1)} %all_gather.27, bf16[3696,2048]{1,0:T(8,128)(2,1)} %param.45), kind=kOutput, calls=%fused_computation.249 | convolution fusion | flops 1937768448 | bytes 17133568 | tf_op jit(solution)/shard_map/dot_general | solution.py:190
  342.3 8.5 %psum.30 = f32[16]{0:T(128)S(1)} all-reduce(f32[16]{0:T(128)S(1)} %get-tuple-element.503), channel_id=1, replica_groups=mesh['req'=8,'kv'=4] {'kv'}, use_global_device_ids=true, to_apply=%region_12.17 | all-reduce | flops 16 | bytes 128 | tf_op jit(solution)/shard_map/psum | solution.py:49
  350.9 11.0 %all_gather.28 = bf16[16,8192]{1,0:T(8,128)(2,1)S(1)} all-gather(bf16[16,2048]{1,0:T(8,128)(2,1)S(1)} %multiply_convert_fusion.1), channel_id=1, replica_groups=mesh['req'=8,'kv'=4] {'kv'}, dimensions={1}, use_global_device_ids=true | all-gather | bytes 327680 | tf_op jit(solution)/shard_map/all_gather | solution.py:26
  361.9 13.6 %all_to_all.76 = bf16[16,8,1024]{2,0,1:T(8,128)(2,1)S(1)} all-to-all(bf16[16,8,1024]{2,0,1:T(8,128)(2,1)S(1)} %bitcast.369), channel_id=1, replica_groups=mesh['req'=8,'kv'=4] {'req'}, dimensions={1} | all-to-all | bytes 524288 | tf_op jit(solution)/shard_map/all_to_all | solution.py:27
  390.9 6.4 copy.108
  397.4 6.5 copy.109
  404.7 46.4 %while.39 = (s32[]{:T(128)}, f32[16,2,8]{0,2,1:T(8,128)S(1)}, f32[16,2,8]{0,2,1:T(8,128)S(1)}, f32[16,2,8,128]{3,0,2,1:T(8,128)S(1)}, s32[16]{0:T(128)S(1)}, /*i...) while((s32[]{:T(128)}, f32[16,2,8]{0,2,1:T(8,128)S(1)}, ...), condition=%wide.region_17.22_spmd.clone, body=%wide.region_14.21_spmd.clone.sunk | while | flops 68379904 | bytes 2478401 | solution.py:94
  451.3 11.5 %all_gather.29 = bf16[16,8192]{1,0:T(8,128)(2,1)S(1)} all-gather(bf16[16,2048]{1,0:T(8,128)(2,1)S(1)} %bitcast.372), channel_id=1, replica_groups=mesh['req'=8,'kv'=4] {'kv'}, dimensions={1}, use_global_device_ids=true | all-gather | bytes 327680 | tf_op jit(solution)/shard_map/all_gather | solution.py:26
  462.8 11.2 %all_to_all.77 = bf16[16,8,1024]{2,0,1:T(8,128)(2,1)S(1)} all-to-all(bf16[16,8,1024]{2,0,1:T(8,128)(2,1)S(1)} %bitcast.370), channel_id=1, replica_groups=mesh['req'=8,'kv'=4] {'req'}, dimensions={1} | all-to-all | bytes 524288 | tf_op jit(solution)/shard_map/all_to_all | solution.py:27
  493.9 6.9 %psum.31 = f32[16]{0:T(128)S(1)} all-reduce(f32[16]{0:T(128)S(1)} %get-tuple-element.501), channel_id=1, replica_groups=mesh['req'=8,'kv'=4] {'kv'}, use_global_device_ids=true, to_apply=%region_19.24 | all-reduce | flops 16 | bytes 128 | tf_op jit(solution)/shard_map/psum | solution.py:49
  500.9 10.7 %all_gather.30 = bf16[128,2048]{1,0:T(8,128)(2,1)S(1)} all-gather(bf16[16,2048]{1,0:T(8,128)(2,1)S(1)} %multiply_convert_fusion), channel_id=1, replica_groups=mesh['req'=8,'kv'=4] {'req'}, dimensions={0}, use_global_device_ids=true | all-gather | bytes 589824 | tf_op jit(solution)/shard_map/all_gather | solution.py:171
  511.6 7.6 %fusion.115 = f32[128,3696]{0,1:T(8,128)S(1)} fusion(bf16[128,2048]{1,0:T(8,128)(2,1)S(1)} %all_gather.30, bf16[2048,3696]{0,1:T(8,128)(2,1)} %param.43), kind=kOutput, calls=%fused_computation.250 | convolution fusion | flops 1937768448 | bytes 17555456 | tf_op jit(solution)/shard_map/dot_general | solution.py:176
  519.2 7.6 %fusion.116 = f32[128,3696]{0,1:T(8,128)S(1)} fusion(bf16[128,2048]{1,0:T(8,128)(2,1)S(1)} %all_gather.30, bf16[2048,3696]{0,1:T(8,128)(2,1)} %param.44), kind=kOutput, calls=%fused_computation.251 | convolution fusion | flops 1937768448 | bytes 17555456 | tf_op jit(solution)/shard_map/dot_general | solution.py:177
  534.2 68.5 %reduce-scatter.9.cloned.1.call-done = f32[32,7392]{1,0:T(8,128)} async-done(((f32[128,7392]{1,0:T(8,128)}), f32[32,7392]{1,0:T(8,128)}) %reduce-scatter.9.cloned.1.call-update) | async-done | bytes 946192 | tf_op jit(solution)/shard_map/reduce_scatter | solution.py:173
  604.1 19.4 %all_gather.31 = bf16[128,3696]{1,0:T(8,128)(2,1)S(1)} all-gather(bf16[32,3696]{1,0:T(8,128)(2,1)S(1)} %fusion.32), channel_id=1, replica_groups=mesh['req'=8,'kv'=4] {'kv'}, dimensions={0}, use_global_device_ids=true | all-gather | bytes 1182720 | tf_op jit(solution)/shard_map/all_gather | solution.py:188
  623.6 7.7 %fusion.117 = f32[128,2048]{1,0:T(8,128)S(1)} fusion(bf16[128,3696]{1,0:T(8,128)(2,1)S(1)} %all_gather.31, bf16[3696,2048]{1,0:T(8,128)(2,1)} %param.45), kind=kOutput, calls=%fused_computation.252 | convolution fusion | flops 1937768448 | bytes 17133568 | tf_op jit(solution)/shard_map/dot_general | solution.py:190
  (468 shorter events, 237.4 us)
Async XLA Ops:
  31.7 33.3 %all-to-all-start = ((bf16[16,8,1024]{2,0,1:T(8,128)(2,1)}), bf16[16,8,1024]{2,0,1:T(8,128)(2,1)S(1)}, u32[]{:S(2)}, u32[]{:S(2)}) async-start(bf16[16,8,1024]{2,0,1:T(8,128)(2,1)} %bitcast.324), calls=%async_computation | async-start | bytes 524288 | tf_op jit(solution)/shard_map/all_to_all | solution.py:27
  72.4 19.2 %collective-permute-start.2 = (f32[16,2560]{1,0:T(8,128)S(1)}, f32[16,2560]{1,0:T(8,128)S(1)}, u32[]{:S(2)}, u32[]{:S(2)}) collective-permute-start(f32[16,2560]{1,0:T(8,128)S(1)} %get-tuple-element.527), channel_id=1, source_target_pairs={{0,12},{4,16},{8,20},{12,24},{16,28},{20,0},{24,4},{28,8},{1,13},{... | collective-permute-start | bytes 491528 | tf_op jit(solution)/shard_map/ppermute | solution.py:21
  72.9 18.8 %collective-permute-start.3 = (f32[16,2560]{1,0:T(8,128)S(1)}, f32[16,2560]{1,0:T(8,128)S(1)}, u32[]{:S(2)}, u32[]{:S(2)}) collective-permute-start(f32[16,2560]{1,0:T(8,128)S(1)} %get-tuple-element.526), channel_id=1, source_target_pairs={{0,16},{4,20},{8,24},{12,28},{16,0},{20,4},{24,8},{28,12},{1,17},{... | collective-permute-start | bytes 491528 | tf_op jit(solution)/shard_map/ppermute | solution.py:21
  73.2 18.5 %collective-permute-start.4 = (f32[16,2560]{1,0:T(8,128)S(1)}, f32[16,2560]{1,0:T(8,128)S(1)}, u32[]{:S(2)}, u32[]{:S(2)}) collective-permute-start(f32[16,2560]{1,0:T(8,128)S(1)} %get-tuple-element.525), channel_id=1, source_target_pairs={{0,20},{4,24},{8,28},{12,0},{16,4},{20,8},{24,12},{28,16},{1,21},{... | collective-permute-start | bytes 491528 | tf_op jit(solution)/shard_map/ppermute | solution.py:21
  75.4 16.3 %collective-permute-start.5 = (f32[16,2560]{1,0:T(8,128)S(1)}, f32[16,2560]{1,0:T(8,128)S(1)}, u32[]{:S(2)}, u32[]{:S(2)}) collective-permute-start(f32[16,2560]{1,0:T(8,128)S(1)} %get-tuple-element.524), channel_id=1, source_target_pairs={{0,24},{4,28},{8,0},{12,4},{16,8},{20,12},{24,16},{28,20},{1,25},{... | collective-permute-start | bytes 491528 | tf_op jit(solution)/shard_map/ppermute | solution.py:21
  78.8 12.9 %collective-permute-start.6 = (f32[16,2560]{1,0:T(8,128)S(1)}, f32[16,2560]{1,0:T(8,128)S(1)}, u32[]{:S(2)}, u32[]{:S(2)}) collective-permute-start(f32[16,2560]{1,0:T(8,128)S(1)} %get-tuple-element.523), channel_id=1, source_target_pairs={{0,28},{4,0},{8,4},{12,8},{16,12},{20,16},{24,20},{28,24},{1,29},{... | collective-permute-start | bytes 491528 | tf_op jit(solution)/shard_map/ppermute | solution.py:21
  151.2 14.1 %all-to-all-start.1 = ((bf16[16,8,1024]{2,0,1:T(8,128)(2,1)}), bf16[16,8,1024]{2,0,1:T(8,128)(2,1)S(1)}, u32[]{:S(2)}, u32[]{:S(2)}) async-start(bf16[16,8,1024]{2,0,1:T(8,128)(2,1)} %bitcast.323), calls=%async_computation.1 | async-start | bytes 524288 | tf_op jit(solution)/shard_map/all_to_all | solution.py:27
  159.7 137.0 %reduce-scatter.7.cloned.1.call-start = ((), (), s32[]{:S(2)}) async-start(), calls=%async_computation.6 | async-start | bytes 4751360 | tf_op jit(solution)/shard_map/reduce_scatter | solution.py:173
  172.3 8.4 %collective-permute-start.12 = (f32[16,2048]{1,0:T(8,128)S(1)}, f32[16,2048]{1,0:T(8,128)S(1)}, u32[]{:S(2)}, u32[]{:S(2)}) collective-permute-start(f32[16,2048]{1,0:T(8,128)S(1)} %get-tuple-element.552), channel_id=1, source_target_pairs={{0,24},{4,28},{8,0},{12,4},{16,8},{20,12},{24,16},{28,20},{1,25},{... | collective-permute-start | bytes 393224 | tf_op jit(solution)/shard_map/ppermute | solution.py:21
  175.3 9.3 %collective-permute-start.8 = (f32[16,2048]{1,0:T(8,128)S(1)}, f32[16,2048]{1,0:T(8,128)S(1)}, u32[]{:S(2)}, u32[]{:S(2)}) collective-permute-start(f32[16,2048]{1,0:T(8,128)S(1)} %get-tuple-element.556), channel_id=1, source_target_pairs={{0,8},{4,12},{8,16},{12,20},{16,24},{20,28},{24,0},{28,4},{1,9},{5... | collective-permute-start | bytes 393224 | tf_op jit(solution)/shard_map/ppermute | solution.py:21
  176.7 9.1 %collective-permute-start.9 = (f32[16,2048]{1,0:T(8,128)S(1)}, f32[16,2048]{1,0:T(8,128)S(1)}, u32[]{:S(2)}, u32[]{:S(2)}) collective-permute-start(f32[16,2048]{1,0:T(8,128)S(1)} %get-tuple-element.555), channel_id=1, source_target_pairs={{0,12},{4,16},{8,20},{12,24},{16,28},{20,0},{24,4},{28,8},{1,13},{... | collective-permute-start | bytes 393224 | tf_op jit(solution)/shard_map/ppermute | solution.py:21
  228.9 373.9 %reduce-scatter.9.cloned.1.call-start = ((), (), s32[]{:S(2)}) async-start(), calls=%async_computation.7 | async-start | bytes 4751360 | tf_op jit(solution)/shard_map/reduce_scatter | solution.py:173
  329.9 8.6 %collective-permute-start.16 = (f32[16,2048]{1,0:T(8,128)S(1)}, f32[16,2048]{1,0:T(8,128)S(1)}, u32[]{:S(2)}, u32[]{:S(2)}) collective-permute-start(f32[16,2048]{1,0:T(8,128)S(1)} %get-tuple-element.548), channel_id=1, source_target_pairs={{0,12},{4,16},{8,20},{12,24},{16,28},{20,0},{24,4},{28,8},{1,13},{... | collective-permute-start | bytes 393224 | tf_op jit(solution)/shard_map/ppermute | solution.py:21
  330.2 11.5 %collective-permute-start.17 = (f32[16,2048]{1,0:T(8,128)S(1)}, f32[16,2048]{1,0:T(8,128)S(1)}, u32[]{:S(2)}, u32[]{:S(2)}) collective-permute-start(f32[16,2048]{1,0:T(8,128)S(1)} %get-tuple-element.547), channel_id=1, source_target_pairs={{0,16},{4,20},{8,24},{12,28},{16,0},{20,4},{24,8},{28,12},{1,17},{... | collective-permute-start | bytes 393224 | tf_op jit(solution)/shard_map/ppermute | solution.py:21
  330.5 11.3 %collective-permute-start.18 = (f32[16,2048]{1,0:T(8,128)S(1)}, f32[16,2048]{1,0:T(8,128)S(1)}, u32[]{:S(2)}, u32[]{:S(2)}) collective-permute-start(f32[16,2048]{1,0:T(8,128)S(1)} %get-tuple-element.546), channel_id=1, source_target_pairs={{0,20},{4,24},{8,28},{12,0},{16,4},{20,8},{24,12},{28,16},{1,21},{... | collective-permute-start | bytes 393224 | tf_op jit(solution)/shard_map/ppermute | solution.py:21
  332.9 8.9 %collective-permute-start.19 = (f32[16,2048]{1,0:T(8,128)S(1)}, f32[16,2048]{1,0:T(8,128)S(1)}, u32[]{:S(2)}, u32[]{:S(2)}) collective-permute-start(f32[16,2048]{1,0:T(8,128)S(1)} %get-tuple-element.545), channel_id=1, source_target_pairs={{0,24},{4,28},{8,0},{12,4},{16,8},{20,12},{24,16},{28,20},{1,25},{... | collective-permute-start | bytes 393224 | tf_op jit(solution)/shard_map/ppermute | solution.py:21
  381.4 9.6 %collective-permute-start.22 = (f32[16,2560]{1,0:T(8,128)S(1)}, f32[16,2560]{1,0:T(8,128)S(1)}, u32[]{:S(2)}, u32[]{:S(2)}) collective-permute-start(f32[16,2560]{1,0:T(8,128)S(1)} %get-tuple-element.521), channel_id=1, source_target_pairs={{0,8},{4,12},{8,16},{12,20},{16,24},{20,28},{24,0},{28,4},{1,9},{5... | collective-permute-start | bytes 491528 | tf_op jit(solution)/shard_map/ppermute | solution.py:21
  382.6 21.3 %collective-permute-start.23 = (f32[16,2560]{1,0:T(8,128)S(1)}, f32[16,2560]{1,0:T(8,128)S(1)}, u32[]{:S(2)}, u32[]{:S(2)}) collective-permute-start(f32[16,2560]{1,0:T(8,128)S(1)} %get-tuple-element.520), channel_id=1, source_target_pairs={{0,12},{4,16},{8,20},{12,24},{16,28},{20,0},{24,4},{28,8},{1,13},{... | collective-permute-start | bytes 491528 | tf_op jit(solution)/shard_map/ppermute | solution.py:21
  382.6 21.3 %collective-permute-start.24 = (f32[16,2560]{1,0:T(8,128)S(1)}, f32[16,2560]{1,0:T(8,128)S(1)}, u32[]{:S(2)}, u32[]{:S(2)}) collective-permute-start(f32[16,2560]{1,0:T(8,128)S(1)} %get-tuple-element.519), channel_id=1, source_target_pairs={{0,16},{4,20},{8,24},{12,28},{16,0},{20,4},{24,8},{28,12},{1,17},{... | collective-permute-start | bytes 491528 | tf_op jit(solution)/shard_map/ppermute | solution.py:21
  383.7 20.1 %collective-permute-start.25 = (f32[16,2560]{1,0:T(8,128)S(1)}, f32[16,2560]{1,0:T(8,128)S(1)}, u32[]{:S(2)}, u32[]{:S(2)}) collective-permute-start(f32[16,2560]{1,0:T(8,128)S(1)} %get-tuple-element.518), channel_id=1, source_target_pairs={{0,20},{4,24},{8,28},{12,0},{16,4},{20,8},{24,12},{28,16},{1,21},{... | collective-permute-start | bytes 491528 | tf_op jit(solution)/shard_map/ppermute | solution.py:21
  386.7 17.2 %collective-permute-start.26 = (f32[16,2560]{1,0:T(8,128)S(1)}, f32[16,2560]{1,0:T(8,128)S(1)}, u32[]{:S(2)}, u32[]{:S(2)}) collective-permute-start(f32[16,2560]{1,0:T(8,128)S(1)} %get-tuple-element.517), channel_id=1, source_target_pairs={{0,24},{4,28},{8,0},{12,4},{16,8},{20,12},{24,16},{28,20},{1,25},{... | collective-permute-start | bytes 491528 | tf_op jit(solution)/shard_map/ppermute | solution.py:21
  390.9 12.9 %collective-permute-start.27 = (f32[16,2560]{1,0:T(8,128)S(1)}, f32[16,2560]{1,0:T(8,128)S(1)}, u32[]{:S(2)}, u32[]{:S(2)}) collective-permute-start(f32[16,2560]{1,0:T(8,128)S(1)} %get-tuple-element.516), channel_id=1, source_target_pairs={{0,28},{4,0},{8,4},{12,8},{16,12},{20,16},{24,20},{28,24},{1,29},{... | collective-permute-start | bytes 491528 | tf_op jit(solution)/shard_map/ppermute | solution.py:21
  479.5 8.2 %collective-permute-start.29 = (f32[16,2048]{1,0:T(8,128)S(1)}, f32[16,2048]{1,0:T(8,128)S(1)}, u32[]{:S(2)}, u32[]{:S(2)}) collective-permute-start(f32[16,2048]{1,0:T(8,128)S(1)} %get-tuple-element.542), channel_id=1, source_target_pairs={{0,8},{4,12},{8,16},{12,20},{16,24},{20,28},{24,0},{28,4},{1,9},{5... | collective-permute-start | bytes 393224 | tf_op jit(solution)/shard_map/ppermute | solution.py:21
  480.6 8.6 %collective-permute-start.30 = (f32[16,2048]{1,0:T(8,128)S(1)}, f32[16,2048]{1,0:T(8,128)S(1)}, u32[]{:S(2)}, u32[]{:S(2)}) collective-permute-start(f32[16,2048]{1,0:T(8,128)S(1)} %get-tuple-element.541), channel_id=1, source_target_pairs={{0,12},{4,16},{8,20},{12,24},{16,28},{20,0},{24,4},{28,8},{1,13},{... | collective-permute-start | bytes 393224 | tf_op jit(solution)/shard_map/ppermute | solution.py:21
  480.6 13.0 %collective-permute-start.31 = (f32[16,2048]{1,0:T(8,128)S(1)}, f32[16,2048]{1,0:T(8,128)S(1)}, u32[]{:S(2)}, u32[]{:S(2)}) collective-permute-start(f32[16,2048]{1,0:T(8,128)S(1)} %get-tuple-element.540), channel_id=1, source_target_pairs={{0,16},{4,20},{8,24},{12,28},{16,0},{20,4},{24,8},{28,12},{1,17},{... | collective-permute-start | bytes 393224 | tf_op jit(solution)/shard_map/ppermute | solution.py:21
  481.8 11.9 %collective-permute-start.32 = (f32[16,2048]{1,0:T(8,128)S(1)}, f32[16,2048]{1,0:T(8,128)S(1)}, u32[]{:S(2)}, u32[]{:S(2)}) collective-permute-start(f32[16,2048]{1,0:T(8,128)S(1)} %get-tuple-element.539), channel_id=1, source_target_pairs={{0,20},{4,24},{8,28},{12,0},{16,4},{20,8},{24,12},{28,16},{1,21},{... | collective-permute-start | bytes 393224 | tf_op jit(solution)/shard_map/ppermute | solution.py:21
  484.8 9.0 %collective-permute-start.33 = (f32[16,2048]{1,0:T(8,128)S(1)}, f32[16,2048]{1,0:T(8,128)S(1)}, u32[]{:S(2)}, u32[]{:S(2)}) collective-permute-start(f32[16,2048]{1,0:T(8,128)S(1)} %get-tuple-element.538), channel_id=1, source_target_pairs={{0,24},{4,28},{8,0},{12,4},{16,8},{20,12},{24,16},{28,20},{1,25},{... | collective-permute-start | bytes 393224 | tf_op jit(solution)/shard_map/ppermute | solution.py:21
  631.4 7.8 %collective-permute-start.35 = (f32[16,2048]{1,0:T(8,128)S(1)}, f32[16,2048]{1,0:T(8,128)S(1)}, u32[]{:S(2)}, u32[]{:S(2)}) collective-permute-start(f32[16,2048]{1,0:T(8,128)S(1)} %get-tuple-element.529), channel_id=1, source_target_pairs={{0,4},{4,8},{8,12},{12,16},{16,20},{20,24},{24,28},{28,0},{1,5},{5... | collective-permute-start | bytes 393224 | tf_op jit(solution)/shard_map/ppermute | solution.py:21
  636.2 8.6 %collective-permute-start.37 = (f32[16,2048]{1,0:T(8,128)S(1)}, f32[16,2048]{1,0:T(8,128)S(1)}, u32[]{:S(2)}, u32[]{:S(2)}) collective-permute-start(f32[16,2048]{1,0:T(8,128)S(1)} %get-tuple-element.534), channel_id=1, source_target_pairs={{0,12},{4,16},{8,20},{12,24},{16,28},{20,0},{24,4},{28,8},{1,13},{... | collective-permute-start | bytes 393224 | tf_op jit(solution)/shard_map/ppermute | solution.py:21
  636.6 11.4 %collective-permute-start.38 = (f32[16,2048]{1,0:T(8,128)S(1)}, f32[16,2048]{1,0:T(8,128)S(1)}, u32[]{:S(2)}, u32[]{:S(2)}) collective-permute-start(f32[16,2048]{1,0:T(8,128)S(1)} %get-tuple-element.533), channel_id=1, source_target_pairs={{0,16},{4,20},{8,24},{12,28},{16,0},{20,4},{24,8},{28,12},{1,17},{... | collective-permute-start | bytes 393224 | tf_op jit(solution)/shard_map/ppermute | solution.py:21
  636.8 11.3 %collective-permute-start.39 = (f32[16,2048]{1,0:T(8,128)S(1)}, f32[16,2048]{1,0:T(8,128)S(1)}, u32[]{:S(2)}, u32[]{:S(2)}) collective-permute-start(f32[16,2048]{1,0:T(8,128)S(1)} %get-tuple-element.532), channel_id=1, source_target_pairs={{0,20},{4,24},{8,28},{12,0},{16,4},{20,8},{24,12},{28,16},{1,21},{... | collective-permute-start | bytes 393224 | tf_op jit(solution)/shard_map/ppermute | solution.py:21
  639.2 8.9 %collective-permute-start.40 = (f32[16,2048]{1,0:T(8,128)S(1)}, f32[16,2048]{1,0:T(8,128)S(1)}, u32[]{:S(2)}, u32[]{:S(2)}) collective-permute-start(f32[16,2048]{1,0:T(8,128)S(1)} %get-tuple-element.531), channel_id=1, source_target_pairs={{0,24},{4,28},{8,0},{12,4},{16,8},{20,12},{24,16},{28,20},{1,25},{... | collective-permute-start | bytes 393224 | tf_op jit(solution)/shard_map/ppermute | solution.py:21
  (23 other events, 171.5 us)
Sparse Core Ops, SparseCore 0:
  229.0 67.6 reduce-scatter.6
  534.3 68.3 reduce-scatter.8
where the time goes:
time: 660 us; the launch traced here: 656 us
  waiting for transfers between devices  178 us (27%)
  blocking collectives  165 us (25%)
  matrix products  139 us (21%)
  starting transfers between devices  68.6 us (10%)
  local copies, waits for them, and re-layouts  61.5 us (9%)
  other arithmetic  27.8 us (4%)
  between operations  14 us (2%)
    reduce_scatter x2, waiting for transfers between devices, body(): lax.psum_scatter(jnp.concatenate([jnp.dot(tokens, w_gate, preferred_eleme...  136 us
    ppermute x42, starting transfers between devices, scatter_sum(): lax.ppermute(piece, axis, [(j, (j + shift) % count) for j in range(count)])  50.9 us
    all_gather x4, blocking collectives, rows_for_weights(): wide = lax.all_gather(block, 'kv', axis=1, tiled=True)  45 us
    unnamed x34, local copies, waits for them, and re-layouts  42.2 us
    dot_general x32, matrix products, one_block(): jnp.einsum('igrt,tgd->igrd', exps.astype(jnp.bfloat16), value_block, pref...  40.3 us
    dot_general x32, matrix products, one_block(): jnp.einsum('igrd,tgd->igrt', query_rows, key_block, preferred_element_typ...  39.8 us
    all_gather x2, blocking collectives, body(): hidden_all = lax.all_gather(local_hidden, 'kv', axis=0, tiled=True)  38.6 us
    ppermute x42, waiting for transfers between devices, scatter_sum(): lax.ppermute(piece, axis, [(j, (j + shift) % count) for j in range(count)])  35.8 us
  transfers between devices with their start and end apart: 46, of which 22 were waited for; matrix products, arithmetic and copies ran while one was open for 8% of the time, Pallas kernels for 0%

commit v1 on v0

--- a/solution.py
+++ b/solution.py
@@ -24,7 +24,10 @@
 
 def rows_for_weights(block):
     wide = lax.all_gather(block, "kv", axis=1, tiled=True)
-    return lax.all_to_all(wide, "req", 1, 0, tiled=True)
+    return jnp.concatenate(
+        lax.all_to_all(jnp.stack(jnp.split(wide, lax.axis_size("req"), axis=1)), "req", 0, 0),
+        axis=0,
+    )
 
 
 def apply_rotation(values, token_positions):

time: 660 us -> 668 us (1.012)
  local copies, waits for them, and re-layouts: 61.5 us -> 69.9 us
    unnamed x34 -> x62, local copies, waits for them, and re-layouts: 42.2 us -> 50.8 us
where the time goes in v1:
time: 668 us; the launch traced here: 664 us
  waiting for transfers between devices  178 us (27%)
  blocking collectives  165 us (25%)
  matrix products  139 us (21%)
  local copies, waits for them, and re-layouts  69.9 us (10%)
  starting transfers between devices  68.7 us (10%)
  other arithmetic  27.8 us (4%)
  between operations  14.1 us (2%)
    reduce_scatter x2, waiting for transfers between devices, body(): lax.psum_scatter(jnp.concatenate([jnp.dot(tokens, w_gate, preferred_eleme...  137 us
    ppermute x42, starting transfers between devices, scatter_sum(): lax.ppermute(piece, axis, [(j, (j + shift) % count) for j in range(count)])  51 us
    unnamed x62, local copies, waits for them, and re-layouts  50.8 us
    all_gather x4, blocking collectives, rows_for_weights(): wide = lax.all_gather(block, 'kv', axis=1, tiled=True)  44.9 us
    dot_general x32, matrix products, one_block(): jnp.einsum('igrt,tgd->igrd', exps.astype(jnp.bfloat16), value_block, pref...  40.3 us
    dot_general x32, matrix products, one_block(): jnp.einsum('igrd,tgd->igrt', query_rows, key_block, preferred_element_typ...  39.8 us
    all_gather x2, blocking collectives, body(): hidden_all = lax.all_gather(local_hidden, 'kv', axis=0, tiled=True)  38.6 us
    ppermute x42, waiting for transfers between devices, scatter_sum(): lax.ppermute(piece, axis, [(j, (j + shift) % count) for j in range(count)])  35.8 us
  transfers between devices with their start and end apart: 46, of which 22 were waited for; matrix products, arithmetic and copies ran while one was open for 8% of the time, Pallas kernels for 0%

profile of v1, /device:TPU:1, one launch (start us, length us, event | category | flops | bytes accessed | tf_op | source)
XLA Modules:
  0.0 664.4 jit_solution(7859480288248829355)
XLA Ops:
  8.2 10.8 %psum.28 = f32[16]{0:T(128)S(1)} all-reduce(f32[16]{0:T(128)S(1)} %fusion.60), channel_id=1, replica_groups=mesh['req'=8,'kv'=4] {'kv'}, use_global_device_ids=true, to_apply=%region_1.2 | all-reduce | flops 16 | bytes 128 | tf_op jit(solution)/shard_map/psum | solution.py:52
  19.9 11.1 %all_gather.24 = bf16[16,8192]{1,0:T(8,128)(2,1)S(1)} all-gather(bf16[16,2048]{1,0:T(8,128)(2,1)S(1)} %fusion.62), channel_id=1, replica_groups=mesh['req'=8,'kv'=4] {'kv'}, dimensions={1}, use_global_device_ids=true | all-gather | bytes 327680 | tf_op jit(solution)/shard_map/all_gather | solution.py:26
  35.9 9.2 %all-to-all-start = ((bf16[8,16,1024]{2,1,0:T(8,128)(2,1)}), bf16[8,16,1024]{2,1,0:T(8,128)(2,1)S(1)}, u32[]{:S(2)}, u32[]{:S(2)}) async-start(bf16[8,16,1024]{2,1,0:T(8,128)(2,1)} %constant_dynamic-update-slice_fusion), calls=%async_computation | async-start | bytes 524288 | tf_op jit(solution)/shard_map/all_to_all | solution.py:28
  52.7 5.7 fusion.111
  58.4 5.9 fusion.110
  83.0 6.4 copy.92
  89.4 6.5 copy.93
  96.8 46.3 %while.38 = (s32[]{:T(128)}, f32[16,2,8]{0,2,1:T(8,128)S(1)}, f32[16,2,8]{0,2,1:T(8,128)S(1)}, f32[16,2,8,128]{3,0,2,1:T(8,128)S(1)}, s32[16]{0:T(128)S(1)}, /*i...) while((s32[]{:T(128)}, f32[16,2,8]{0,2,1:T(8,128)S(1)}, ...), condition=%wide.region_6.10_spmd.clone, body=%wide.region_3.9_spmd.clone.sunk | while | flops 68379904 | bytes 2478401 | solution.py:97
  143.3 11.3 %all_gather.25 = bf16[16,8192]{1,0:T(8,128)(2,1)S(1)} all-gather(bf16[16,2048]{1,0:T(8,128)(2,1)S(1)} %bitcast.469), channel_id=1, replica_groups=mesh['req'=8,'kv'=4] {'kv'}, dimensions={1}, use_global_device_ids=true | all-gather | bytes 327680 | tf_op jit(solution)/shard_map/all_gather | solution.py:26
  159.5 8.6 %all-to-all-start.1 = ((bf16[8,16,1024]{2,1,0:T(8,128)(2,1)}), bf16[8,16,1024]{2,1,0:T(8,128)(2,1)S(1)}, u32[]{:S(2)}, u32[]{:S(2)}) async-start(bf16[8,16,1024]{2,1,0:T(8,128)(2,1)} %constant_dynamic-update-slice_fusion.11), calls=%async_computation.1 | async-start | bytes 524288 | tf_op jit(solution)/shard_map/all_to_all | solution.py:28
  194.4 6.9 %psum.29 = f32[16]{0:T(128)S(1)} all-reduce(f32[16]{0:T(128)S(1)} %get-tuple-element.505), channel_id=1, replica_groups=mesh['req'=8,'kv'=4] {'kv'}, use_global_device_ids=true, to_apply=%region_9.14 | all-reduce | flops 16 | bytes 128 | tf_op jit(solution)/shard_map/psum | solution.py:52
  201.4 13.0 %all_gather.26 = bf16[128,2048]{1,0:T(8,128)(2,1)S(1)} all-gather(bf16[16,2048]{1,0:T(8,128)(2,1)S(1)} %multiply_convert_fusion.2), channel_id=1, replica_groups=mesh['req'=8,'kv'=4] {'req'}, dimensions={0}, use_global_device_ids=true | all-gather | bytes 589824 | tf_op jit(solution)/shard_map/all_gather | solution.py:174
  214.3 7.6 %fusion.112 = f32[128,3696]{0,1:T(8,128)S(1)} fusion(bf16[128,2048]{1,0:T(8,128)(2,1)S(1)} %all_gather.26, bf16[2048,3696]{0,1:T(8,128)(2,1)} %param.43), kind=kOutput, calls=%fused_computation.307 | convolution fusion | flops 1937768448 | bytes 17555456 | tf_op jit(solution)/shard_map/dot_general | solution.py:179
  222.0 7.6 %fusion.113 = f32[128,3696]{0,1:T(8,128)S(1)} fusion(bf16[128,2048]{1,0:T(8,128)(2,1)S(1)} %all_gather.26, bf16[2048,3696]{0,1:T(8,128)(2,1)} %param.44), kind=kOutput, calls=%fused_computation.308 | convolution fusion | flops 1937768448 | bytes 17555456 | tf_op jit(solution)/shard_map/dot_general | solution.py:180
  237.1 68.0 %reduce-scatter.7.cloned.1.call-done = f32[32,7392]{1,0:T(8,128)} async-done(((f32[128,7392]{1,0:T(8,128)}), f32[32,7392]{1,0:T(8,128)}) %reduce-scatter.7.cloned.1.call-update) | async-done | bytes 946192 | tf_op jit(solution)/shard_map/reduce_scatter | solution.py:176
  306.4 19.2 %all_gather.27 = bf16[128,3696]{1,0:T(8,128)(2,1)S(1)} all-gather(bf16[32,3696]{1,0:T(8,128)(2,1)S(1)} %fusion.33), channel_id=1, replica_groups=mesh['req'=8,'kv'=4] {'kv'}, dimensions={0}, use_global_device_ids=true | all-gather | bytes 1182720 | tf_op jit(solution)/shard_map/all_gather | solution.py:191
  325.6 7.7 %fusion.114 = f32[128,2048]{1,0:T(8,128)S(1)} fusion(bf16[128,3696]{1,0:T(8,128)(2,1)S(1)} %all_gather.27, bf16[3696,2048]{1,0:T(8,128)(2,1)} %param.45), kind=kOutput, calls=%fused_computation.309 | convolution fusion | flops 1937768448 | bytes 17133568 | tf_op jit(solution)/shard_map/dot_general | solution.py:193
  350.6 8.5 %psum.30 = f32[16]{0:T(128)S(1)} all-reduce(f32[16]{0:T(128)S(1)} %get-tuple-element.503), channel_id=1, replica_groups=mesh['req'=8,'kv'=4] {'kv'}, use_global_device_ids=true, to_apply=%region_12.17 | all-reduce | flops 16 | bytes 128 | tf_op jit(solution)/shard_map/psum | solution.py:52
  359.2 11.0 %all_gather.28 = bf16[16,8192]{1,0:T(8,128)(2,1)S(1)} all-gather(bf16[16,2048]{1,0:T(8,128)(2,1)S(1)} %multiply_convert_fusion.1), channel_id=1, replica_groups=mesh['req'=8,'kv'=4] {'kv'}, dimensions={1}, use_global_device_ids=true | all-gather | bytes 327680 | tf_op jit(solution)/shard_map/all_gather | solution.py:26
  370.3 13.5 %all_to_all.20 = bf16[8,16,1024]{2,1,0:T(8,128)(2,1)S(1)} all-to-all(bf16[8,16,1024]{2,1,0:T(8,128)(2,1)S(1)} %constant_dynamic-update-slice_fusion.19), channel_id=1, replica_groups=mesh['req'=8,'kv'=4] {'req'}, dimensions={0} | all-to-all | bytes 524288 | tf_op jit(solution)/shard_map/all_to_all | solution.py:28
  399.2 6.4 copy.94
  405.7 6.5 copy.95
  413.0 46.4 %while.39 = (s32[]{:T(128)}, f32[16,2,8]{0,2,1:T(8,128)S(1)}, f32[16,2,8]{0,2,1:T(8,128)S(1)}, f32[16,2,8,128]{3,0,2,1:T(8,128)S(1)}, s32[16]{0:T(128)S(1)}, /*i...) while((s32[]{:T(128)}, f32[16,2,8]{0,2,1:T(8,128)S(1)}, ...), condition=%wide.region_17.22_spmd.clone, body=%wide.region_14.21_spmd.clone.sunk | while | flops 68379904 | bytes 2478401 | solution.py:97
  459.6 11.5 %all_gather.29 = bf16[16,8192]{1,0:T(8,128)(2,1)S(1)} all-gather(bf16[16,2048]{1,0:T(8,128)(2,1)S(1)} %bitcast.470), channel_id=1, replica_groups=mesh['req'=8,'kv'=4] {'kv'}, dimensions={1}, use_global_device_ids=true | all-gather | bytes 327680 | tf_op jit(solution)/shard_map/all_gather | solution.py:26
  471.1 11.2 %all_to_all.21 = bf16[8,16,1024]{2,1,0:T(8,128)(2,1)S(1)} all-to-all(bf16[8,16,1024]{2,1,0:T(8,128)(2,1)S(1)} %constant_dynamic-update-slice_fusion.27), channel_id=1, replica_groups=mesh['req'=8,'kv'=4] {'req'}, dimensions={0} | all-to-all | bytes 524288 | tf_op jit(solution)/shard_map/all_to_all | solution.py:28
  502.3 6.8 %psum.31 = f32[16]{0:T(128)S(1)} all-reduce(f32[16]{0:T(128)S(1)} %get-tuple-element.501), channel_id=1, replica_groups=mesh['req'=8,'kv'=4] {'kv'}, use_global_device_ids=true, to_apply=%region_19.24 | all-reduce | flops 16 | bytes 128 | tf_op jit(solution)/shard_map/psum | solution.py:52
  509.2 10.7 %all_gather.30 = bf16[128,2048]{1,0:T(8,128)(2,1)S(1)} all-gather(bf16[16,2048]{1,0:T(8,128)(2,1)S(1)} %multiply_convert_fusion), channel_id=1, replica_groups=mesh['req'=8,'kv'=4] {'req'}, dimensions={0}, use_global_device_ids=true | all-gather | bytes 589824 | tf_op jit(solution)/shard_map/all_gather | solution.py:174
  519.9 7.6 %fusion.115 = f32[128,3696]{0,1:T(8,128)S(1)} fusion(bf16[128,2048]{1,0:T(8,128)(2,1)S(1)} %all_gather.30, bf16[2048,3696]{0,1:T(8,128)(2,1)} %param.43), kind=kOutput, calls=%fused_computation.310 | convolution fusion | flops 1937768448 | bytes 17555456 | tf_op jit(solution)/shard_map/dot_general | solution.py:179
  527.6 7.6 %fusion.116 = f32[128,3696]{0,1:T(8,128)S(1)} fusion(bf16[128,2048]{1,0:T(8,128)(2,1)S(1)} %all_gather.30, bf16[2048,3696]{0,1:T(8,128)(2,1)} %param.44), kind=kOutput, calls=%fused_computation.311 | convolution fusion | flops 1937768448 | bytes 17555456 | tf_op jit(solution)/shard_map/dot_general | solution.py:180
  542.6 68.5 %reduce-scatter.9.cloned.1.call-done = f32[32,7392]{1,0:T(8,128)} async-done(((f32[128,7392]{1,0:T(8,128)}), f32[32,7392]{1,0:T(8,128)}) %reduce-scatter.9.cloned.1.call-update) | async-done | bytes 946192 | tf_op jit(solution)/shard_map/reduce_scatter | solution.py:176
  612.5 19.4 %all_gather.31 = bf16[128,3696]{1,0:T(8,128)(2,1)S(1)} all-gather(bf16[32,3696]{1,0:T(8,128)(2,1)S(1)} %fusion.32), channel_id=1, replica_groups=mesh['req'=8,'kv'=4] {'kv'}, dimensions={0}, use_global_device_ids=true | all-gather | bytes 1182720 | tf_op jit(solution)/shard_map/all_gather | solution.py:191
  631.9 7.7 %fusion.117 = f32[128,2048]{1,0:T(8,128)S(1)} fusion(bf16[128,3696]{1,0:T(8,128)(2,1)S(1)} %all_gather.31, bf16[3696,2048]{1,0:T(8,128)(2,1)} %param.45), kind=kOutput, calls=%fused_computation.312 | convolution fusion | flops 1937768448 | bytes 17133568 | tf_op jit(solution)/shard_map/dot_general | solution.py:193
  (496 shorter events, 245.8 us)
Async XLA Ops:
  35.9 33.3 %all-to-all-start = ((bf16[8,16,1024]{2,1,0:T(8,128)(2,1)}), bf16[8,16,1024]{2,1,0:T(8,128)(2,1)S(1)}, u32[]{:S(2)}, u32[]{:S(2)}) async-start(bf16[8,16,1024]{2,1,0:T(8,128)(2,1)} %constant_dynamic-update-slice_fusion), calls=%async_computation | async-start | bytes 524288 | tf_op jit(solution)/shard_map/all_to_all | solution.py:28
  76.6 19.2 %collective-permute-start.2 = (f32[16,2560]{1,0:T(8,128)S(1)}, f32[16,2560]{1,0:T(8,128)S(1)}, u32[]{:S(2)}, u32[]{:S(2)}) collective-permute-start(f32[16,2560]{1,0:T(8,128)S(1)} %get-tuple-element.527), channel_id=1, source_target_pairs={{0,12},{4,16},{8,20},{12,24},{16,28},{20,0},{24,4},{28,8},{1,13},{... | collective-permute-start | bytes 491528 | tf_op jit(solution)/shard_map/ppermute | solution.py:21
  77.1 18.8 %collective-permute-start.3 = (f32[16,2560]{1,0:T(8,128)S(1)}, f32[16,2560]{1,0:T(8,128)S(1)}, u32[]{:S(2)}, u32[]{:S(2)}) collective-permute-start(f32[16,2560]{1,0:T(8,128)S(1)} %get-tuple-element.526), channel_id=1, source_target_pairs={{0,16},{4,20},{8,24},{12,28},{16,0},{20,4},{24,8},{28,12},{1,17},{... | collective-permute-start | bytes 491528 | tf_op jit(solution)/shard_map/ppermute | solution.py:21
  77.4 18.5 %collective-permute-start.4 = (f32[16,2560]{1,0:T(8,128)S(1)}, f32[16,2560]{1,0:T(8,128)S(1)}, u32[]{:S(2)}, u32[]{:S(2)}) collective-permute-start(f32[16,2560]{1,0:T(8,128)S(1)} %get-tuple-element.525), channel_id=1, source_target_pairs={{0,20},{4,24},{8,28},{12,0},{16,4},{20,8},{24,12},{28,16},{1,21},{... | collective-permute-start | bytes 491528 | tf_op jit(solution)/shard_map/ppermute | solution.py:21
  79.6 16.3 %collective-permute-start.5 = (f32[16,2560]{1,0:T(8,128)S(1)}, f32[16,2560]{1,0:T(8,128)S(1)}, u32[]{:S(2)}, u32[]{:S(2)}) collective-permute-start(f32[16,2560]{1,0:T(8,128)S(1)} %get-tuple-element.524), channel_id=1, source_target_pairs={{0,24},{4,28},{8,0},{12,4},{16,8},{20,12},{24,16},{28,20},{1,25},{... | collective-permute-start | bytes 491528 | tf_op jit(solution)/shard_map/ppermute | solution.py:21
  83.0 12.9 %collective-permute-start.6 = (f32[16,2560]{1,0:T(8,128)S(1)}, f32[16,2560]{1,0:T(8,128)S(1)}, u32[]{:S(2)}, u32[]{:S(2)}) collective-permute-start(f32[16,2560]{1,0:T(8,128)S(1)} %get-tuple-element.523), channel_id=1, source_target_pairs={{0,28},{4,0},{8,4},{12,8},{16,12},{20,16},{24,20},{28,24},{1,29},{... | collective-permute-start | bytes 491528 | tf_op jit(solution)/shard_map/ppermute | solution.py:21
  159.5 14.2 %all-to-all-start.1 = ((bf16[8,16,1024]{2,1,0:T(8,128)(2,1)}), bf16[8,16,1024]{2,1,0:T(8,128)(2,1)S(1)}, u32[]{:S(2)}, u32[]{:S(2)}) async-start(bf16[8,16,1024]{2,1,0:T(8,128)(2,1)} %constant_dynamic-update-slice_fusion.11), calls=%async_computation.1 | async-start | bytes 524288 | tf_op jit(solution)/shard_map/all_to_all | solution.py:28
  168.1 137.0 %reduce-scatter.7.cloned.1.call-start = ((), (), s32[]{:S(2)}) async-start(), calls=%async_computation.6 | async-start | bytes 4751360 | tf_op jit(solution)/shard_map/reduce_scatter | solution.py:176
  180.7 8.4 %collective-permute-start.12 = (f32[16,2048]{1,0:T(8,128)S(1)}, f32[16,2048]{1,0:T(8,128)S(1)}, u32[]{:S(2)}, u32[]{:S(2)}) collective-permute-start(f32[16,2048]{1,0:T(8,128)S(1)} %get-tuple-element.552), channel_id=1, source_target_pairs={{0,24},{4,28},{8,0},{12,4},{16,8},{20,12},{24,16},{28,20},{1,25},{... | collective-permute-start | bytes 393224 | tf_op jit(solution)/shard_map/ppermute | solution.py:21
  183.6 9.3 %collective-permute-start.8 = (f32[16,2048]{1,0:T(8,128)S(1)}, f32[16,2048]{1,0:T(8,128)S(1)}, u32[]{:S(2)}, u32[]{:S(2)}) collective-permute-start(f32[16,2048]{1,0:T(8,128)S(1)} %get-tuple-element.556), channel_id=1, source_target_pairs={{0,8},{4,12},{8,16},{12,20},{16,24},{20,28},{24,0},{28,4},{1,9},{5... | collective-permute-start | bytes 393224 | tf_op jit(solution)/shard_map/ppermute | solution.py:21
  185.1 9.1 %collective-permute-start.9 = (f32[16,2048]{1,0:T(8,128)S(1)}, f32[16,2048]{1,0:T(8,128)S(1)}, u32[]{:S(2)}, u32[]{:S(2)}) collective-permute-start(f32[16,2048]{1,0:T(8,128)S(1)} %get-tuple-element.555), channel_id=1, source_target_pairs={{0,12},{4,16},{8,20},{12,24},{16,28},{20,0},{24,4},{28,8},{1,13},{... | collective-permute-start | bytes 393224 | tf_op jit(solution)/shard_map/ppermute | solution.py:21
  237.0 374.1 %reduce-scatter.9.cloned.1.call-start = ((), (), s32[]{:S(2)}) async-start(), calls=%async_computation.7 | async-start | bytes 4751360 | tf_op jit(solution)/shard_map/reduce_scatter | solution.py:176
  333.4 7.8 %collective-permute-start.14 = (f32[16,2048]{1,0:T(8,128)S(1)}, f32[16,2048]{1,0:T(8,128)S(1)}, u32[]{:S(2)}, u32[]{:S(2)}) collective-permute-start(f32[16,2048]{1,0:T(8,128)S(1)} %get-tuple-element.543), channel_id=1, source_target_pairs={{0,4},{4,8},{8,12},{12,16},{16,20},{20,24},{24,28},{28,0},{1,5},{5... | collective-permute-start | bytes 393224 | tf_op jit(solution)/shard_map/ppermute | solution.py:21
  338.2 8.6 %collective-permute-start.16 = (f32[16,2048]{1,0:T(8,128)S(1)}, f32[16,2048]{1,0:T(8,128)S(1)}, u32[]{:S(2)}, u32[]{:S(2)}) collective-permute-start(f32[16,2048]{1,0:T(8,128)S(1)} %get-tuple-element.548), channel_id=1, source_target_pairs={{0,12},{4,16},{8,20},{12,24},{16,28},{20,0},{24,4},{28,8},{1,13},{... | collective-permute-start | bytes 393224 | tf_op jit(solution)/shard_map/ppermute | solution.py:21
  338.6 11.4 %collective-permute-start.17 = (f32[16,2048]{1,0:T(8,128)S(1)}, f32[16,2048]{1,0:T(8,128)S(1)}, u32[]{:S(2)}, u32[]{:S(2)}) collective-permute-start(f32[16,2048]{1,0:T(8,128)S(1)} %get-tuple-element.547), channel_id=1, source_target_pairs={{0,16},{4,20},{8,24},{12,28},{16,0},{20,4},{24,8},{28,12},{1,17},{... | collective-permute-start | bytes 393224 | tf_op jit(solution)/shard_map/ppermute | solution.py:21
  338.9 11.3 %collective-permute-start.18 = (f32[16,2048]{1,0:T(8,128)S(1)}, f32[16,2048]{1,0:T(8,128)S(1)}, u32[]{:S(2)}, u32[]{:S(2)}) collective-permute-start(f32[16,2048]{1,0:T(8,128)S(1)} %get-tuple-element.546), channel_id=1, source_target_pairs={{0,20},{4,24},{8,28},{12,0},{16,4},{20,8},{24,12},{28,16},{1,21},{... | collective-permute-start | bytes 393224 | tf_op jit(solution)/shard_map/ppermute | solution.py:21
  341.3 8.9 %collective-permute-start.19 = (f32[16,2048]{1,0:T(8,128)S(1)}, f32[16,2048]{1,0:T(8,128)S(1)}, u32[]{:S(2)}, u32[]{:S(2)}) collective-permute-start(f32[16,2048]{1,0:T(8,128)S(1)} %get-tuple-element.545), channel_id=1, source_target_pairs={{0,24},{4,28},{8,0},{12,4},{16,8},{20,12},{24,16},{28,20},{1,25},{... | collective-permute-start | bytes 393224 | tf_op jit(solution)/shard_map/ppermute | solution.py:21
  389.7 9.6 %collective-permute-start.22 = (f32[16,2560]{1,0:T(8,128)S(1)}, f32[16,2560]{1,0:T(8,128)S(1)}, u32[]{:S(2)}, u32[]{:S(2)}) collective-permute-start(f32[16,2560]{1,0:T(8,128)S(1)} %get-tuple-element.521), channel_id=1, source_target_pairs={{0,8},{4,12},{8,16},{12,20},{16,24},{20,28},{24,0},{28,4},{1,9},{5... | collective-permute-start | bytes 491528 | tf_op jit(solution)/shard_map/ppermute | solution.py:21
  390.9 21.3 %collective-permute-start.23 = (f32[16,2560]{1,0:T(8,128)S(1)}, f32[16,2560]{1,0:T(8,128)S(1)}, u32[]{:S(2)}, u32[]{:S(2)}) collective-permute-start(f32[16,2560]{1,0:T(8,128)S(1)} %get-tuple-element.520), channel_id=1, source_target_pairs={{0,12},{4,16},{8,20},{12,24},{16,28},{20,0},{24,4},{28,8},{1,13},{... | collective-permute-start | bytes 491528 | tf_op jit(solution)/shard_map/ppermute | solution.py:21
  390.9 21.3 %collective-permute-start.24 = (f32[16,2560]{1,0:T(8,128)S(1)}, f32[16,2560]{1,0:T(8,128)S(1)}, u32[]{:S(2)}, u32[]{:S(2)}) collective-permute-start(f32[16,2560]{1,0:T(8,128)S(1)} %get-tuple-element.519), channel_id=1, source_target_pairs={{0,16},{4,20},{8,24},{12,28},{16,0},{20,4},{24,8},{28,12},{1,17},{... | collective-permute-start | bytes 491528 | tf_op jit(solution)/shard_map/ppermute | solution.py:21
  392.0 20.1 %collective-permute-start.25 = (f32[16,2560]{1,0:T(8,128)S(1)}, f32[16,2560]{1,0:T(8,128)S(1)}, u32[]{:S(2)}, u32[]{:S(2)}) collective-permute-start(f32[16,2560]{1,0:T(8,128)S(1)} %get-tuple-element.518), channel_id=1, source_target_pairs={{0,20},{4,24},{8,28},{12,0},{16,4},{20,8},{24,12},{28,16},{1,21},{... | collective-permute-start | bytes 491528 | tf_op jit(solution)/shard_map/ppermute | solution.py:21
  395.0 17.2 %collective-permute-start.26 = (f32[16,2560]{1,0:T(8,128)S(1)}, f32[16,2560]{1,0:T(8,128)S(1)}, u32[]{:S(2)}, u32[]{:S(2)}) collective-permute-start(f32[16,2560]{1,0:T(8,128)S(1)} %get-tuple-element.517), channel_id=1, source_target_pairs={{0,24},{4,28},{8,0},{12,4},{16,8},{20,12},{24,16},{28,20},{1,25},{... | collective-permute-start | bytes 491528 | tf_op jit(solution)/shard_map/ppermute | solution.py:21
  399.2 12.9 %collective-permute-start.27 = (f32[16,2560]{1,0:T(8,128)S(1)}, f32[16,2560]{1,0:T(8,128)S(1)}, u32[]{:S(2)}, u32[]{:S(2)}) collective-permute-start(f32[16,2560]{1,0:T(8,128)S(1)} %get-tuple-element.516), channel_id=1, source_target_pairs={{0,28},{4,0},{8,4},{12,8},{16,12},{20,16},{24,20},{28,24},{1,29},{... | collective-permute-start | bytes 491528 | tf_op jit(solution)/shard_map/ppermute | solution.py:21
  487.8 8.2 %collective-permute-start.29 = (f32[16,2048]{1,0:T(8,128)S(1)}, f32[16,2048]{1,0:T(8,128)S(1)}, u32[]{:S(2)}, u32[]{:S(2)}) collective-permute-start(f32[16,2048]{1,0:T(8,128)S(1)} %get-tuple-element.542), channel_id=1, source_target_pairs={{0,8},{4,12},{8,16},{12,20},{16,24},{20,28},{24,0},{28,4},{1,9},{5... | collective-permute-start | bytes 393224 | tf_op jit(solution)/shard_map/ppermute | solution.py:21
  489.0 8.6 %collective-permute-start.30 = (f32[16,2048]{1,0:T(8,128)S(1)}, f32[16,2048]{1,0:T(8,128)S(1)}, u32[]{:S(2)}, u32[]{:S(2)}) collective-permute-start(f32[16,2048]{1,0:T(8,128)S(1)} %get-tuple-element.541), channel_id=1, source_target_pairs={{0,12},{4,16},{8,20},{12,24},{16,28},{20,0},{24,4},{28,8},{1,13},{... | collective-permute-start | bytes 393224 | tf_op jit(solution)/shard_map/ppermute | solution.py:21
  489.0 13.0 %collective-permute-start.31 = (f32[16,2048]{1,0:T(8,128)S(1)}, f32[16,2048]{1,0:T(8,128)S(1)}, u32[]{:S(2)}, u32[]{:S(2)}) collective-permute-start(f32[16,2048]{1,0:T(8,128)S(1)} %get-tuple-element.540), channel_id=1, source_target_pairs={{0,16},{4,20},{8,24},{12,28},{16,0},{20,4},{24,8},{28,12},{1,17},{... | collective-permute-start | bytes 393224 | tf_op jit(solution)/shard_map/ppermute | solution.py:21
  490.2 11.9 %collective-permute-start.32 = (f32[16,2048]{1,0:T(8,128)S(1)}, f32[16,2048]{1,0:T(8,128)S(1)}, u32[]{:S(2)}, u32[]{:S(2)}) collective-permute-start(f32[16,2048]{1,0:T(8,128)S(1)} %get-tuple-element.539), channel_id=1, source_target_pairs={{0,20},{4,24},{8,28},{12,0},{16,4},{20,8},{24,12},{28,16},{1,21},{... | collective-permute-start | bytes 393224 | tf_op jit(solution)/shard_map/ppermute | solution.py:21
  493.1 9.0 %collective-permute-start.33 = (f32[16,2048]{1,0:T(8,128)S(1)}, f32[16,2048]{1,0:T(8,128)S(1)}, u32[]{:S(2)}, u32[]{:S(2)}) collective-permute-start(f32[16,2048]{1,0:T(8,128)S(1)} %get-tuple-element.538), channel_id=1, source_target_pairs={{0,24},{4,28},{8,0},{12,4},{16,8},{20,12},{24,16},{28,20},{1,25},{... | collective-permute-start | bytes 393224 | tf_op jit(solution)/shard_map/ppermute | solution.py:21
  644.6 8.6 %collective-permute-start.37 = (f32[16,2048]{1,0:T(8,128)S(1)}, f32[16,2048]{1,0:T(8,128)S(1)}, u32[]{:S(2)}, u32[]{:S(2)}) collective-permute-start(f32[16,2048]{1,0:T(8,128)S(1)} %get-tuple-element.534), channel_id=1, source_target_pairs={{0,12},{4,16},{8,20},{12,24},{16,28},{20,0},{24,4},{28,8},{1,13},{... | collective-permute-start | bytes 393224 | tf_op jit(solution)/shard_map/ppermute | solution.py:21
  644.9 11.4 %collective-permute-start.38 = (f32[16,2048]{1,0:T(8,128)S(1)}, f32[16,2048]{1,0:T(8,128)S(1)}, u32[]{:S(2)}, u32[]{:S(2)}) collective-permute-start(f32[16,2048]{1,0:T(8,128)S(1)} %get-tuple-element.533), channel_id=1, source_target_pairs={{0,16},{4,20},{8,24},{12,28},{16,0},{20,4},{24,8},{28,12},{1,17},{... | collective-permute-start | bytes 393224 | tf_op jit(solution)/shard_map/ppermute | solution.py:21
  645.2 11.2 %collective-permute-start.39 = (f32[16,2048]{1,0:T(8,128)S(1)}, f32[16,2048]{1,0:T(8,128)S(1)}, u32[]{:S(2)}, u32[]{:S(2)}) collective-permute-start(f32[16,2048]{1,0:T(8,128)S(1)} %get-tuple-element.532), channel_id=1, source_target_pairs={{0,20},{4,24},{8,28},{12,0},{16,4},{20,8},{24,12},{28,16},{1,21},{... | collective-permute-start | bytes 393224 | tf_op jit(solution)/shard_map/ppermute | solution.py:21
  647.5 8.9 %collective-permute-start.40 = (f32[16,2048]{1,0:T(8,128)S(1)}, f32[16,2048]{1,0:T(8,128)S(1)}, u32[]{:S(2)}, u32[]{:S(2)}) collective-permute-start(f32[16,2048]{1,0:T(8,128)S(1)} %get-tuple-element.531), channel_id=1, source_target_pairs={{0,24},{4,28},{8,0},{12,4},{16,8},{20,12},{24,16},{28,20},{1,25},{... | collective-permute-start | bytes 393224 | tf_op jit(solution)/shard_map/ppermute | solution.py:21
  (23 other events, 171.5 us)
Sparse Core Ops, SparseCore 0:
  237.1 67.9 reduce-scatter.6
  542.7 68.3 reduce-scatter.8
